TPU v7x, 512 devices: a whole 4x4x16 slice. The times are simulated.
512 devices in a mesh: band: 8 (over x_lo, y), xy: 64 (over z, x_hi, core).
Axes of the slice: x: 4 (x_hi: 2, x_lo: 2; x = x_hi * 2 + x_lo), y: 4, z: 16, core: 2. Of those that a mesh axis runs over, the one named last changes fastest.
Arguments:
- orbitals: float32 [16, 64, 128, 256], P('band', 'xy'), may hold values from -6 to 6
- energies: float32 [16], P('band'), may hold values from -1.5 to -0.25
- occupation: int32 [16], P('band'), may hold values from 1 to 2
- potential: float32 [64, 128, 256], P('xy'), may hold values from 0.25 to 2
- trials: float32 [4, 64, 128, 256], P(None, 'xy'), may hold values from -8 to 23
Outputs:
- density: float32 [4, 64, 128, 256], P(None, 'xy', 'band')
- response_matrix: float32 [4, 4], replicated
All inputs are finite; a program needn't handle non-finite values.
Results may differ from a plain program's by a relative error of at most 0.0001.
Values sent between devices are 32-bit elements; how exact they have to be, the bound alone decides.
No kernel may reach another device: no remote copies, remote signals or barrier semaphores. Data moves between devices by JAX's collectives and lax.ppermute only.
A program may use at most 64 MiB of HBM per device.

v0:
```python
import math
import jax
import jax.numpy as jnp
from jax import lax
from jax.sharding import PartitionSpec as P

ITERS = 3


def padded_2(block, sides, width):
    for axis, dim in sides:
        count = lax.axis_size(axis)
        forward = [(i, i + 1) for i in range(count - 1)]
        forward.append((count - 1, 0))
        backward = [(target, source) for source, target in forward]
        low = lax.ppermute(
            lax.slice_in_dim(block, block.shape[dim] - width, None, axis=dim), axis, forward
        )
        high = lax.ppermute(lax.slice_in_dim(block, 0, width, axis=dim), axis, backward)
        block = jnp.concatenate([low, block, high], axis=dim)
    return block


def tree_sum(value, axes):
    for axis in axes:
        count = lax.axis_size(axis)
        step = 1
        while step < count:
            pairs = [(i, i ^ step) for i in range(count)]
            value = value + lax.ppermute(value, axis, pairs)
            step *= 2
    return value


def respond(psi_rows, energy_rows, weight_rows, potential_part, trial_part, project, apply_op):
    orbital_count, cell_count = psi_rows.shape
    trial_count = trial_part.shape[0]
    row_count = orbital_count * trial_count
    diagonal_op = 3.0 + potential_part.reshape(1, 1, cell_count) - energy_rows[:, None, None]
    diagonal_op = jnp.broadcast_to(diagonal_op, (orbital_count, trial_count, cell_count)).reshape(
        row_count, cell_count
    )
    products = trial_part[None, :, :] * psi_rows[:, None, :]
    right_side = -project(products.reshape(row_count, cell_count))
    update = project(right_side / diagonal_op)
    for iteration in range(ITERS):
        residual = right_side - apply_op(update, diagonal_op)
        update = update + project(residual / diagonal_op)
    weights = weight_rows[:, None, None] * psi_rows[:, None, :]
    return jnp.sum(weights * update.reshape(orbital_count, trial_count, cell_count), axis=0)


def neighbours_z(field_block):
    z_padded = jnp.pad(field_block, ((0, 0), (0, 0), (0, 0), (1, 1)))
    return z_padded[..., 2:] + z_padded[..., :-2]


def local(orbitals, energies, occupation, potential, trials):
    nb_dev, width_x, width_y, width_z = orbitals.shape
    trial_count = trials.shape[0]
    cell_count = width_x * width_y * width_z
    cell_total = cell_count * lax.axis_size("xy")
    orbital_total = nb_dev * lax.axis_size("band")
    y_share = width_y // lax.axis_size("band")
    band_index = lax.axis_index("band")
    highest = lax.Precision.HIGHEST
    trial_slice = lax.dynamic_slice_in_dim(trials, band_index * y_share, y_share, 2)
    psi_flat = orbitals.reshape(nb_dev, cell_count)
    psi_all = lax.all_gather(psi_flat, "band", axis=0, tiled=True)

    def project_slab(vectors):
        intersection = jnp.dot(
            psi_all, vectors.T, precision=highest, preferred_element_type=jnp.float32
        )
        intersection = tree_sum(intersection, ("xy",)) / cell_total
        return vectors - jnp.dot(
            intersection.T, psi_all, precision=highest, preferred_element_type=jnp.float32
        )

    def apply_slab(vectors, diagonal_op):
        field_block = vectors.reshape(-1, width_x, width_y, width_z)
        padded = padded_2(field_block, (("xy", 1),), 1)
        beside = padded[:, 2:] + padded[:, :-2]
        beside = beside + jnp.roll(field_block, 1, 2) + jnp.roll(field_block, -1, 2)
        beside = beside + neighbours_z(field_block)
        return diagonal_op * vectors - 0.5 * beside.reshape(vectors.shape)

    summed = respond(
        psi_flat,
        energies,
        occupation.astype(jnp.float32),
        potential.reshape(cell_count),
        trials.reshape(trial_count, cell_count),
        project_slab,
        apply_slab,
    )
    partial_grid = (summed / math.sqrt(orbital_total)).reshape(
        trial_count, width_x, width_y, width_z
    )
    density = lax.psum_scatter(partial_grid, "band", scatter_dimension=2, tiled=True)
    local_sum = jnp.dot(
        density.reshape(trial_count, -1),
        trial_slice.reshape(trial_count, -1).T,
        precision=highest,
        preferred_element_type=jnp.float32,
    )
    response_matrix = tree_sum(local_sum, ("band", "xy")) / cell_total
    return (density, response_matrix)


def solution(mesh):
    in_specs = (
        P("band", "xy", None, None),
        P("band"),
        P("band"),
        P("xy", None, None),
        P(None, "xy", None, None),
    )
    out_specs = (P(None, "xy", "band", None), P())
    return jax.shard_map(local, mesh=mesh, in_specs=in_specs, out_specs=out_specs, check_vma=False)
```

profile of v0, /device:TPU:4, one launch (start us, length us, event | category | flops | bytes accessed | tf_op | source)
XLA Modules:
  0.0 520.0 jit_solution(7207219664055754807)
XLA Ops:
  12.3 50.8 %all-gather.3.cloned.1.call-done = f32[8,2,32768]{2,1,0:T(2,128)} async-done(((f32[1,2,32768]{2,1,0:T(2,128)}), f32[8,2,32768]{2,1,0:T(2,128)}) %all-gather.3.cloned.1.call-update) | async-done | bytes 2097168 | tf_op jit(solution)/shard_map/all_gather | solution.py:69
  74.2 4.2 collective-permute-done.1
  78.4 3.5 collective-permute-start.2
  83.9 4.4 collective-permute-start.3
  90.3 7.6 %collective-permute-start.4 = (f32[16,8]{0,1:T(8,128)S(1)}, f32[16,8]{0,1:T(8,128)S(1)}, u32[]{:S(2)}, u32[]{:S(2)}) collective-permute-start(f32[16,8]{0,1:T(8,128)S(1)} %add.199), channel_id=1, source_target_pairs={{0,16},{1,17},{2,18},{3,19},{4,20},{5,21},{6,22},{7,23},{8,24},{9,... | collective-permute-start | bytes 1544 | tf_op jit(solution)/shard_map/ppermute | solution.py:30
  99.7 12.8 %collective-permute-start.5 = (f32[16,8]{0,1:T(8,128)S(1)}, f32[16,8]{0,1:T(8,128)S(1)}, u32[]{:S(2)}, u32[]{:S(2)}) collective-permute-start(f32[16,8]{0,1:T(8,128)S(1)} %add.200), channel_id=1, source_target_pairs={{0,32},{1,33},{2,34},{3,35},{4,36},{5,37},{6,38},{7,39},{8,40},{9,... | collective-permute-start | bytes 1544 | tf_op jit(solution)/shard_map/ppermute | solution.py:30
  126.3 4.2 collective-permute-done.7
  133.1 2.9 collective-permute-done.8
  136.1 2.9 collective-permute-start.9
  139.0 3.5 collective-permute-done.9
  142.5 6.0 %collective-permute-start.10 = (f32[16,8]{0,1:T(8,128)S(1)}, f32[16,8]{0,1:T(8,128)S(1)}, u32[]{:S(2)}, u32[]{:S(2)}) collective-permute-start(f32[16,8]{0,1:T(8,128)S(1)} %add.208), channel_id=1, source_target_pairs={{0,16},{1,17},{2,18},{3,19},{4,20},{5,21},{6,22},{7,23},{8,24},{9,... | collective-permute-start | bytes 1544 | tf_op jit(solution)/shard_map/ppermute | solution.py:30
  148.5 3.3 collective-permute-done.10
  151.9 11.2 %collective-permute-start.11 = (f32[16,8]{0,1:T(8,128)S(1)}, f32[16,8]{0,1:T(8,128)S(1)}, u32[]{:S(2)}, u32[]{:S(2)}) collective-permute-start(f32[16,8]{0,1:T(8,128)S(1)} %add.209), channel_id=1, source_target_pairs={{0,32},{1,33},{2,34},{3,35},{4,36},{5,37},{6,38},{7,39},{8,40},{9,... | collective-permute-start | bytes 1544 | tf_op jit(solution)/shard_map/ppermute | solution.py:30
  163.1 3.0 collective-permute-done.11
  171.9 20.8 %collective-permute-done.12 = f32[8,1,128,256]{3,0,2,1:T(8,128)S(1)} collective-permute-done((f32[8,1,128,256]{3,0,2,1:T(8,128)S(1)}, f32[8,1,128,256]{3,0,2,1:T(8,128)S(1)}, u32[]{:S(2)}, u32[]{:S(2)}) %collective-permute-start.12) | collective-permute-done | bytes 1048608 | tf_op jit(solution)/shard_map/ppermute | solution.py:19
  200.5 4.0 collective-permute-start.15
  204.5 3.0 collective-permute-done.15
  207.5 2.8 collective-permute-start.16
  213.0 4.5 collective-permute-start.17
  219.4 7.3 %collective-permute-start.18 = (f32[16,8]{0,1:T(8,128)S(1)}, f32[16,8]{0,1:T(8,128)S(1)}, u32[]{:S(2)}, u32[]{:S(2)}) collective-permute-start(f32[16,8]{0,1:T(8,128)S(1)} %add.219), channel_id=1, source_target_pairs={{0,16},{1,17},{2,18},{3,19},{4,20},{5,21},{6,22},{7,23},{8,24},{9,... | collective-permute-start | bytes 1544 | tf_op jit(solution)/shard_map/ppermute | solution.py:30
  228.8 11.2 %collective-permute-start.19 = (f32[16,8]{0,1:T(8,128)S(1)}, f32[16,8]{0,1:T(8,128)S(1)}, u32[]{:S(2)}, u32[]{:S(2)}) collective-permute-start(f32[16,8]{0,1:T(8,128)S(1)} %add.220), channel_id=1, source_target_pairs={{0,32},{1,33},{2,34},{3,35},{4,36},{5,37},{6,38},{7,39},{8,40},{9,... | collective-permute-start | bytes 1544 | tf_op jit(solution)/shard_map/ppermute | solution.py:30
  240.0 3.0 collective-permute-done.19
  248.8 21.0 %collective-permute-done.20 = f32[8,1,128,256]{3,0,2,1:T(8,128)S(1)} collective-permute-done((f32[8,1,128,256]{3,0,2,1:T(8,128)S(1)}, f32[8,1,128,256]{3,0,2,1:T(8,128)S(1)}, u32[]{:S(2)}, u32[]{:S(2)}) %collective-permute-start.20) | collective-permute-done | bytes 1048608 | tf_op jit(solution)/shard_map/ppermute | solution.py:19
  281.5 4.2 collective-permute-done.23
  285.7 2.8 collective-permute-start.24
  291.2 4.5 collective-permute-start.25
  297.6 7.3 %collective-permute-start.26 = (f32[16,8]{0,1:T(8,128)S(1)}, f32[16,8]{0,1:T(8,128)S(1)}, u32[]{:S(2)}, u32[]{:S(2)}) collective-permute-start(f32[16,8]{0,1:T(8,128)S(1)} %add.231), channel_id=1, source_target_pairs={{0,16},{1,17},{2,18},{3,19},{4,20},{5,21},{6,22},{7,23},{8,24},{9,... | collective-permute-start | bytes 1544 | tf_op jit(solution)/shard_map/ppermute | solution.py:30
  307.0 11.2 %collective-permute-start.27 = (f32[16,8]{0,1:T(8,128)S(1)}, f32[16,8]{0,1:T(8,128)S(1)}, u32[]{:S(2)}, u32[]{:S(2)}) collective-permute-start(f32[16,8]{0,1:T(8,128)S(1)} %add.232), channel_id=1, source_target_pairs={{0,32},{1,33},{2,34},{3,35},{4,36},{5,37},{6,38},{7,39},{8,40},{9,... | collective-permute-start | bytes 1544 | tf_op jit(solution)/shard_map/ppermute | solution.py:30
  318.2 3.0 collective-permute-done.27
  327.0 21.0 %collective-permute-done.28 = f32[8,1,128,256]{3,0,2,1:T(8,128)S(1)} collective-permute-done((f32[8,1,128,256]{3,0,2,1:T(8,128)S(1)}, f32[8,1,128,256]{3,0,2,1:T(8,128)S(1)}, u32[]{:S(2)}, u32[]{:S(2)}) %collective-permute-start.28) | collective-permute-done | bytes 1048608 | tf_op jit(solution)/shard_map/ppermute | solution.py:19
  356.8 2.9 collective-permute-start.31
  359.7 4.1 collective-permute-done.31
  363.8 3.4 collective-permute-start.32
  369.3 4.8 collective-permute-start.33
  375.7 7.6 %collective-permute-start.34 = (f32[16,8]{0,1:T(8,128)S(1)}, f32[16,8]{0,1:T(8,128)S(1)}, u32[]{:S(2)}, u32[]{:S(2)}) collective-permute-start(f32[16,8]{0,1:T(8,128)S(1)} %add.243), channel_id=1, source_target_pairs={{0,16},{1,17},{2,18},{3,19},{4,20},{5,21},{6,22},{7,23},{8,24},{9,... | collective-permute-start | bytes 1544 | tf_op jit(solution)/shard_map/ppermute | solution.py:30
  385.1 10.2 %collective-permute-start.35 = (f32[16,8]{0,1:T(8,128)S(1)}, f32[16,8]{0,1:T(8,128)S(1)}, u32[]{:S(2)}, u32[]{:S(2)}) collective-permute-start(f32[16,8]{0,1:T(8,128)S(1)} %add.244), channel_id=1, source_target_pairs={{0,32},{1,33},{2,34},{3,35},{4,36},{5,37},{6,38},{7,39},{8,40},{9,... | collective-permute-start | bytes 1544 | tf_op jit(solution)/shard_map/ppermute | solution.py:30
  396.1 3.2 collective-permute-done.35
  405.5 42.3 %reduce-scatter.2.cloned.1.call-done = f32[4,1,16,256]{3,2,1,0:T(8,128)} async-done(((f32[4,1,128,256]{3,2,1,0:T(8,128)}), f32[4,1,16,256]{3,2,1,0:T(8,128)}) %reduce-scatter.2.cloned.1.call-update) | async-done | bytes 65552 | tf_op jit(solution)/shard_map/reduce_scatter | solution.py:100
  451.0 3.6 collective-permute-done.36
  454.5 2.8 collective-permute-start.37
  457.3 4.2 collective-permute-done.37
  461.5 2.7 collective-permute-start.38
  470.0 2.8 collective-permute-start.40
  472.8 4.2 collective-permute-done.40
  477.0 3.4 collective-permute-start.41
  482.5 4.4 collective-permute-start.42
  488.8 7.6 %collective-permute-start.43 = (f32[4,4]{1,0:T(4,128)S(1)}, f32[4,4]{1,0:T(4,128)S(1)}, u32[]{:S(2)}, u32[]{:S(2)}) collective-permute-start(f32[4,4]{1,0:T(4,128)S(1)} %add.254), channel_id=1, source_target_pairs={{0,16},{1,17},{2,18},{3,19},{4,20},{5,21},{6,22},{7,23},{8,24},{9,... | collective-permute-start | bytes 200 | tf_op jit(solution)/shard_map/ppermute | solution.py:30
  498.2 12.8 %collective-permute-start.44 = (f32[4,4]{1,0:T(4,128)S(1)}, f32[4,4]{1,0:T(4,128)S(1)}, u32[]{:S(2)}, u32[]{:S(2)}) collective-permute-start(f32[4,4]{1,0:T(4,128)S(1)} %add.255), channel_id=1, source_target_pairs={{0,32},{1,33},{2,34},{3,35},{4,36},{5,37},{6,38},{7,39},{8,40},{9,... | collective-permute-start | bytes 200 | tf_op jit(solution)/shard_map/ppermute | solution.py:30
  (130 shorter events, 126.2 us)
Async XLA Ops:
  7.2 55.9 %all-gather.3.cloned.1.call-start = ((), (), s32[]{:S(2)}) async-start(), calls=%async_computation.2 | async-start | bytes 2359296 | tf_op jit(solution)/shard_map/all_gather | solution.py:69
  9.0 438.7 %reduce-scatter.2.cloned.1.call-start = ((), (), s32[]{:S(2)}) async-start(), calls=%async_computation.1 | async-start | bytes 589824 | tf_op jit(solution)/shard_map/reduce_scatter | solution.py:100
  12.2 100.5 %copy-start = (f32[8,32768]{1,0:T(8,128)}, f32[8,32768]{1,0:T(8,128)S(1)}, u32[]{:S(2)}) copy-start(f32[8,32768]{1,0:T(8,128)S(1)} %mul.77) | copy-start | bytes 3145732
  68.4 3.1 collective-permute-start
  71.4 7.0 %collective-permute-start.1 = (f32[16,8]{0,1:T(8,128)S(1)}, f32[16,8]{0,1:T(8,128)S(1)}, u32[]{:S(2)}, u32[]{:S(2)}) collective-permute-start(f32[16,8]{0,1:T(8,128)S(1)} %add.196), channel_id=1, source_target_pairs={{0,2},{1,3},{2,0},{3,1},{4,6},{5,7},{6,4},{7,5},{8,10},{9,11},{10,... | collective-permute-start | bytes 1544 | tf_op jit(solution)/shard_map/ppermute | solution.py:30
  78.4 5.5 %collective-permute-start.2 = (f32[16,8]{0,1:T(8,128)S(1)}, f32[16,8]{0,1:T(8,128)S(1)}, u32[]{:S(2)}, u32[]{:S(2)}) collective-permute-start(f32[16,8]{0,1:T(8,128)S(1)} %add.197), channel_id=1, source_target_pairs={{0,4},{1,5},{2,6},{3,7},{4,0},{5,1},{6,2},{7,3},{8,12},{9,13},{10,... | collective-permute-start | bytes 1544 | tf_op jit(solution)/shard_map/ppermute | solution.py:30
  83.9 6.4 %collective-permute-start.3 = (f32[16,8]{0,1:T(8,128)S(1)}, f32[16,8]{0,1:T(8,128)S(1)}, u32[]{:S(2)}, u32[]{:S(2)}) collective-permute-start(f32[16,8]{0,1:T(8,128)S(1)} %add.198), channel_id=1, source_target_pairs={{0,8},{1,9},{2,10},{3,11},{4,12},{5,13},{6,14},{7,15},{8,0},{9,1},... | collective-permute-start | bytes 1544 | tf_op jit(solution)/shard_map/ppermute | solution.py:30
  90.3 9.4 %collective-permute-start.4 = (f32[16,8]{0,1:T(8,128)S(1)}, f32[16,8]{0,1:T(8,128)S(1)}, u32[]{:S(2)}, u32[]{:S(2)}) collective-permute-start(f32[16,8]{0,1:T(8,128)S(1)} %add.199), channel_id=1, source_target_pairs={{0,16},{1,17},{2,18},{3,19},{4,20},{5,21},{6,22},{7,23},{8,24},{9,... | collective-permute-start | bytes 1544 | tf_op jit(solution)/shard_map/ppermute | solution.py:30
  99.7 15.8 %collective-permute-start.5 = (f32[16,8]{0,1:T(8,128)S(1)}, f32[16,8]{0,1:T(8,128)S(1)}, u32[]{:S(2)}, u32[]{:S(2)}) collective-permute-start(f32[16,8]{0,1:T(8,128)S(1)} %add.200), channel_id=1, source_target_pairs={{0,32},{1,33},{2,34},{3,35},{4,36},{5,37},{6,38},{7,39},{8,40},{9,... | collective-permute-start | bytes 1544 | tf_op jit(solution)/shard_map/ppermute | solution.py:30
  120.5 3.1 collective-permute-start.6
  123.6 7.0 %collective-permute-start.7 = (f32[16,8]{0,1:T(8,128)S(1)}, f32[16,8]{0,1:T(8,128)S(1)}, u32[]{:S(2)}, u32[]{:S(2)}) collective-permute-start(f32[16,8]{0,1:T(8,128)S(1)} %add.205), channel_id=1, source_target_pairs={{0,2},{1,3},{2,0},{3,1},{4,6},{5,7},{6,4},{7,5},{8,10},{9,11},{10,... | collective-permute-start | bytes 1544 | tf_op jit(solution)/shard_map/ppermute | solution.py:30
  130.6 5.5 %collective-permute-start.8 = (f32[16,8]{0,1:T(8,128)S(1)}, f32[16,8]{0,1:T(8,128)S(1)}, u32[]{:S(2)}, u32[]{:S(2)}) collective-permute-start(f32[16,8]{0,1:T(8,128)S(1)} %add.206), channel_id=1, source_target_pairs={{0,4},{1,5},{2,6},{3,7},{4,0},{5,1},{6,2},{7,3},{8,12},{9,13},{10,... | collective-permute-start | bytes 1544 | tf_op jit(solution)/shard_map/ppermute | solution.py:30
  136.1 6.4 %collective-permute-start.9 = (f32[16,8]{0,1:T(8,128)S(1)}, f32[16,8]{0,1:T(8,128)S(1)}, u32[]{:S(2)}, u32[]{:S(2)}) collective-permute-start(f32[16,8]{0,1:T(8,128)S(1)} %add.207), channel_id=1, source_target_pairs={{0,8},{1,9},{2,10},{3,11},{4,12},{5,13},{6,14},{7,15},{8,0},{9,1},... | collective-permute-start | bytes 1544 | tf_op jit(solution)/shard_map/ppermute | solution.py:30
  142.5 9.4 %collective-permute-start.10 = (f32[16,8]{0,1:T(8,128)S(1)}, f32[16,8]{0,1:T(8,128)S(1)}, u32[]{:S(2)}, u32[]{:S(2)}) collective-permute-start(f32[16,8]{0,1:T(8,128)S(1)} %add.208), channel_id=1, source_target_pairs={{0,16},{1,17},{2,18},{3,19},{4,20},{5,21},{6,22},{7,23},{8,24},{9,... | collective-permute-start | bytes 1544 | tf_op jit(solution)/shard_map/ppermute | solution.py:30
  151.9 14.2 %collective-permute-start.11 = (f32[16,8]{0,1:T(8,128)S(1)}, f32[16,8]{0,1:T(8,128)S(1)}, u32[]{:S(2)}, u32[]{:S(2)}) collective-permute-start(f32[16,8]{0,1:T(8,128)S(1)} %add.209), channel_id=1, source_target_pairs={{0,32},{1,33},{2,34},{3,35},{4,36},{5,37},{6,38},{7,39},{8,40},{9,... | collective-permute-start | bytes 1544 | tf_op jit(solution)/shard_map/ppermute | solution.py:30
  167.2 25.5 %collective-permute-start.12 = (f32[8,1,128,256]{3,0,2,1:T(8,128)S(1)}, f32[8,1,128,256]{3,0,2,1:T(8,128)S(1)}, u32[]{:S(2)}, u32[]{:S(2)}) collective-permute-start(f32[8,1,128,256]{3,0,2,1:T(8,128)S(1)} %bitcast.55), channel_id=1, source_target_pairs={{1,0},{2,1},{3,2},{4,3},{5,4},{6,5},{7,6},{8,7},{9,8},{10,9},{11,1... | collective-permute-start | bytes 3145736 | tf_op jit(solution)/shard_map/ppermute | solution.py:19
  169.2 24.9 %collective-permute-start.13 = (f32[8,1,128,256]{3,0,2,1:T(8,128)S(1)}, f32[8,1,128,256]{3,0,2,1:T(8,128)S(1)}, u32[]{:S(2)}, u32[]{:S(2)}) collective-permute-start(f32[8,1,128,256]{3,0,2,1:T(8,128)S(1)} %bitcast.56), channel_id=1, source_target_pairs={{0,1},{1,2},{2,3},{3,4},{4,5},{5,6},{6,7},{7,8},{8,9},{9,10},{10,1... | collective-permute-start | bytes 3145736 | tf_op jit(solution)/shard_map/ppermute | solution.py:16
  197.4 3.1 collective-permute-start.14
  200.5 7.0 %collective-permute-start.15 = (f32[16,8]{0,1:T(8,128)S(1)}, f32[16,8]{0,1:T(8,128)S(1)}, u32[]{:S(2)}, u32[]{:S(2)}) collective-permute-start(f32[16,8]{0,1:T(8,128)S(1)} %add.216), channel_id=1, source_target_pairs={{0,2},{1,3},{2,0},{3,1},{4,6},{5,7},{6,4},{7,5},{8,10},{9,11},{10,... | collective-permute-start | bytes 1544 | tf_op jit(solution)/shard_map/ppermute | solution.py:30
  207.5 5.5 %collective-permute-start.16 = (f32[16,8]{0,1:T(8,128)S(1)}, f32[16,8]{0,1:T(8,128)S(1)}, u32[]{:S(2)}, u32[]{:S(2)}) collective-permute-start(f32[16,8]{0,1:T(8,128)S(1)} %add.217), channel_id=1, source_target_pairs={{0,4},{1,5},{2,6},{3,7},{4,0},{5,1},{6,2},{7,3},{8,12},{9,13},{10,... | collective-permute-start | bytes 1544 | tf_op jit(solution)/shard_map/ppermute | solution.py:30
  213.0 6.4 %collective-permute-start.17 = (f32[16,8]{0,1:T(8,128)S(1)}, f32[16,8]{0,1:T(8,128)S(1)}, u32[]{:S(2)}, u32[]{:S(2)}) collective-permute-start(f32[16,8]{0,1:T(8,128)S(1)} %add.218), channel_id=1, source_target_pairs={{0,8},{1,9},{2,10},{3,11},{4,12},{5,13},{6,14},{7,15},{8,0},{9,1},... | collective-permute-start | bytes 1544 | tf_op jit(solution)/shard_map/ppermute | solution.py:30
  219.4 9.4 %collective-permute-start.18 = (f32[16,8]{0,1:T(8,128)S(1)}, f32[16,8]{0,1:T(8,128)S(1)}, u32[]{:S(2)}, u32[]{:S(2)}) collective-permute-start(f32[16,8]{0,1:T(8,128)S(1)} %add.219), channel_id=1, source_target_pairs={{0,16},{1,17},{2,18},{3,19},{4,20},{5,21},{6,22},{7,23},{8,24},{9,... | collective-permute-start | bytes 1544 | tf_op jit(solution)/shard_map/ppermute | solution.py:30
  228.8 14.2 %collective-permute-start.19 = (f32[16,8]{0,1:T(8,128)S(1)}, f32[16,8]{0,1:T(8,128)S(1)}, u32[]{:S(2)}, u32[]{:S(2)}) collective-permute-start(f32[16,8]{0,1:T(8,128)S(1)} %add.220), channel_id=1, source_target_pairs={{0,32},{1,33},{2,34},{3,35},{4,36},{5,37},{6,38},{7,39},{8,40},{9,... | collective-permute-start | bytes 1544 | tf_op jit(solution)/shard_map/ppermute | solution.py:30
  244.3 25.5 %collective-permute-start.20 = (f32[8,1,128,256]{3,0,2,1:T(8,128)S(1)}, f32[8,1,128,256]{3,0,2,1:T(8,128)S(1)}, u32[]{:S(2)}, u32[]{:S(2)}) collective-permute-start(f32[8,1,128,256]{3,0,2,1:T(8,128)S(1)} %bitcast.60), channel_id=1, source_target_pairs={{1,0},{2,1},{3,2},{4,3},{5,4},{6,5},{7,6},{8,7},{9,8},{10,9},{11,1... | collective-permute-start | bytes 3145736 | tf_op jit(solution)/shard_map/ppermute | solution.py:19
  246.2 26.1 %collective-permute-start.21 = (f32[8,1,128,256]{3,0,2,1:T(8,128)S(1)}, f32[8,1,128,256]{3,0,2,1:T(8,128)S(1)}, u32[]{:S(2)}, u32[]{:S(2)}) collective-permute-start(f32[8,1,128,256]{3,0,2,1:T(8,128)S(1)} %bitcast.61), channel_id=1, source_target_pairs={{0,1},{1,2},{2,3},{3,4},{4,5},{5,6},{6,7},{7,8},{8,9},{9,10},{10,1... | collective-permute-start | bytes 3145736 | tf_op jit(solution)/shard_map/ppermute | solution.py:16
  275.7 3.1 collective-permute-start.22
  278.7 7.0 %collective-permute-start.23 = (f32[16,8]{0,1:T(8,128)S(1)}, f32[16,8]{0,1:T(8,128)S(1)}, u32[]{:S(2)}, u32[]{:S(2)}) collective-permute-start(f32[16,8]{0,1:T(8,128)S(1)} %add.228), channel_id=1, source_target_pairs={{0,2},{1,3},{2,0},{3,1},{4,6},{5,7},{6,4},{7,5},{8,10},{9,11},{10,... | collective-permute-start | bytes 1544 | tf_op jit(solution)/shard_map/ppermute | solution.py:30
  285.7 5.5 %collective-permute-start.24 = (f32[16,8]{0,1:T(8,128)S(1)}, f32[16,8]{0,1:T(8,128)S(1)}, u32[]{:S(2)}, u32[]{:S(2)}) collective-permute-start(f32[16,8]{0,1:T(8,128)S(1)} %add.229), channel_id=1, source_target_pairs={{0,4},{1,5},{2,6},{3,7},{4,0},{5,1},{6,2},{7,3},{8,12},{9,13},{10,... | collective-permute-start | bytes 1544 | tf_op jit(solution)/shard_map/ppermute | solution.py:30
  291.2 6.4 %collective-permute-start.25 = (f32[16,8]{0,1:T(8,128)S(1)}, f32[16,8]{0,1:T(8,128)S(1)}, u32[]{:S(2)}, u32[]{:S(2)}) collective-permute-start(f32[16,8]{0,1:T(8,128)S(1)} %add.230), channel_id=1, source_target_pairs={{0,8},{1,9},{2,10},{3,11},{4,12},{5,13},{6,14},{7,15},{8,0},{9,1},... | collective-permute-start | bytes 1544 | tf_op jit(solution)/shard_map/ppermute | solution.py:30
  297.6 9.4 %collective-permute-start.26 = (f32[16,8]{0,1:T(8,128)S(1)}, f32[16,8]{0,1:T(8,128)S(1)}, u32[]{:S(2)}, u32[]{:S(2)}) collective-permute-start(f32[16,8]{0,1:T(8,128)S(1)} %add.231), channel_id=1, source_target_pairs={{0,16},{1,17},{2,18},{3,19},{4,20},{5,21},{6,22},{7,23},{8,24},{9,... | collective-permute-start | bytes 1544 | tf_op jit(solution)/shard_map/ppermute | solution.py:30
  307.0 14.2 %collective-permute-start.27 = (f32[16,8]{0,1:T(8,128)S(1)}, f32[16,8]{0,1:T(8,128)S(1)}, u32[]{:S(2)}, u32[]{:S(2)}) collective-permute-start(f32[16,8]{0,1:T(8,128)S(1)} %add.232), channel_id=1, source_target_pairs={{0,32},{1,33},{2,34},{3,35},{4,36},{5,37},{6,38},{7,39},{8,40},{9,... | collective-permute-start | bytes 1544 | tf_op jit(solution)/shard_map/ppermute | solution.py:30
  322.5 25.5 %collective-permute-start.28 = (f32[8,1,128,256]{3,0,2,1:T(8,128)S(1)}, f32[8,1,128,256]{3,0,2,1:T(8,128)S(1)}, u32[]{:S(2)}, u32[]{:S(2)}) collective-permute-start(f32[8,1,128,256]{3,0,2,1:T(8,128)S(1)} %bitcast.50), channel_id=1, source_target_pairs={{1,0},{2,1},{3,2},{4,3},{5,4},{6,5},{7,6},{8,7},{9,8},{10,9},{11,1... | collective-permute-start | bytes 3145736 | tf_op jit(solution)/shard_map/ppermute | solution.py:19
  324.4 26.0 %collective-permute-start.29 = (f32[8,1,128,256]{3,0,2,1:T(8,128)S(1)}, f32[8,1,128,256]{3,0,2,1:T(8,128)S(1)}, u32[]{:S(2)}, u32[]{:S(2)}) collective-permute-start(f32[8,1,128,256]{3,0,2,1:T(8,128)S(1)} %bitcast.51), channel_id=1, source_target_pairs={{0,1},{1,2},{2,3},{3,4},{4,5},{5,6},{6,7},{7,8},{8,9},{9,10},{10,1... | collective-permute-start | bytes 3145736 | tf_op jit(solution)/shard_map/ppermute | solution.py:16
  353.7 3.1 collective-permute-start.30
  356.8 7.0 %collective-permute-start.31 = (f32[16,8]{0,1:T(8,128)S(1)}, f32[16,8]{0,1:T(8,128)S(1)}, u32[]{:S(2)}, u32[]{:S(2)}) collective-permute-start(f32[16,8]{0,1:T(8,128)S(1)} %add.240), channel_id=1, source_target_pairs={{0,2},{1,3},{2,0},{3,1},{4,6},{5,7},{6,4},{7,5},{8,10},{9,11},{10,... | collective-permute-start | bytes 1544 | tf_op jit(solution)/shard_map/ppermute | solution.py:30
  363.8 5.5 %collective-permute-start.32 = (f32[16,8]{0,1:T(8,128)S(1)}, f32[16,8]{0,1:T(8,128)S(1)}, u32[]{:S(2)}, u32[]{:S(2)}) collective-permute-start(f32[16,8]{0,1:T(8,128)S(1)} %add.241), channel_id=1, source_target_pairs={{0,4},{1,5},{2,6},{3,7},{4,0},{5,1},{6,2},{7,3},{8,12},{9,13},{10,... | collective-permute-start | bytes 1544 | tf_op jit(solution)/shard_map/ppermute | solution.py:30
  369.3 6.4 %collective-permute-start.33 = (f32[16,8]{0,1:T(8,128)S(1)}, f32[16,8]{0,1:T(8,128)S(1)}, u32[]{:S(2)}, u32[]{:S(2)}) collective-permute-start(f32[16,8]{0,1:T(8,128)S(1)} %add.242), channel_id=1, source_target_pairs={{0,8},{1,9},{2,10},{3,11},{4,12},{5,13},{6,14},{7,15},{8,0},{9,1},... | collective-permute-start | bytes 1544 | tf_op jit(solution)/shard_map/ppermute | solution.py:30
  375.7 9.4 %collective-permute-start.34 = (f32[16,8]{0,1:T(8,128)S(1)}, f32[16,8]{0,1:T(8,128)S(1)}, u32[]{:S(2)}, u32[]{:S(2)}) collective-permute-start(f32[16,8]{0,1:T(8,128)S(1)} %add.243), channel_id=1, source_target_pairs={{0,16},{1,17},{2,18},{3,19},{4,20},{5,21},{6,22},{7,23},{8,24},{9,... | collective-permute-start | bytes 1544 | tf_op jit(solution)/shard_map/ppermute | solution.py:30
  385.1 14.2 %collective-permute-start.35 = (f32[16,8]{0,1:T(8,128)S(1)}, f32[16,8]{0,1:T(8,128)S(1)}, u32[]{:S(2)}, u32[]{:S(2)}) collective-permute-start(f32[16,8]{0,1:T(8,128)S(1)} %add.244), channel_id=1, source_target_pairs={{0,32},{1,33},{2,34},{3,35},{4,36},{5,37},{6,38},{7,39},{8,40},{9,... | collective-permute-start | bytes 1544 | tf_op jit(solution)/shard_map/ppermute | solution.py:30
  449.0 5.5 %collective-permute-start.36 = (f32[4,4]{1,0:T(4,128)S(1)}, f32[4,4]{1,0:T(4,128)S(1)}, u32[]{:S(2)}, u32[]{:S(2)}) collective-permute-start(f32[4,4]{1,0:T(4,128)S(1)} %convolution_bitcast_fusion.5), channel_id=1, source_target_pairs={{0,64},{64,0},{128,192},{192,128},{256,320},{320,256},{384,448},{4... | collective-permute-start | bytes 200 | tf_op jit(solution)/shard_map/ppermute | solution.py:30
  454.5 7.0 %collective-permute-start.37 = (f32[4,4]{1,0:T(4,128)S(1)}, f32[4,4]{1,0:T(4,128)S(1)}, u32[]{:S(2)}, u32[]{:S(2)}) collective-permute-start(f32[4,4]{1,0:T(4,128)S(1)} %add.248), channel_id=1, source_target_pairs={{0,128},{64,192},{128,0},{192,64},{256,384},{320,448},{384,256},{4... | collective-permute-start | bytes 200 | tf_op jit(solution)/shard_map/ppermute | solution.py:30
  461.5 5.5 %collective-permute-start.38 = (f32[4,4]{1,0:T(4,128)S(1)}, f32[4,4]{1,0:T(4,128)S(1)}, u32[]{:S(2)}, u32[]{:S(2)}) collective-permute-start(f32[4,4]{1,0:T(4,128)S(1)} %add.249), channel_id=1, source_target_pairs={{0,256},{64,320},{128,384},{192,448},{256,0},{320,64},{384,128},{4... | collective-permute-start | bytes 200 | tf_op jit(solution)/shard_map/ppermute | solution.py:30
  467.0 3.0 collective-permute-start.39
  470.0 7.0 %collective-permute-start.40 = (f32[4,4]{1,0:T(4,128)S(1)}, f32[4,4]{1,0:T(4,128)S(1)}, u32[]{:S(2)}, u32[]{:S(2)}) collective-permute-start(f32[4,4]{1,0:T(4,128)S(1)} %add.251), channel_id=1, source_target_pairs={{0,2},{1,3},{2,0},{3,1},{4,6},{5,7},{6,4},{7,5},{8,10},{9,11},{10,... | collective-permute-start | bytes 200 | tf_op jit(solution)/shard_map/ppermute | solution.py:30
  477.0 5.5 %collective-permute-start.41 = (f32[4,4]{1,0:T(4,128)S(1)}, f32[4,4]{1,0:T(4,128)S(1)}, u32[]{:S(2)}, u32[]{:S(2)}) collective-permute-start(f32[4,4]{1,0:T(4,128)S(1)} %add.252), channel_id=1, source_target_pairs={{0,4},{1,5},{2,6},{3,7},{4,0},{5,1},{6,2},{7,3},{8,12},{9,13},{10,... | collective-permute-start | bytes 200 | tf_op jit(solution)/shard_map/ppermute | solution.py:30
  482.5 6.4 %collective-permute-start.42 = (f32[4,4]{1,0:T(4,128)S(1)}, f32[4,4]{1,0:T(4,128)S(1)}, u32[]{:S(2)}, u32[]{:S(2)}) collective-permute-start(f32[4,4]{1,0:T(4,128)S(1)} %add.253), channel_id=1, source_target_pairs={{0,8},{1,9},{2,10},{3,11},{4,12},{5,13},{6,14},{7,15},{8,0},{9,1},... | collective-permute-start | bytes 200 | tf_op jit(solution)/shard_map/ppermute | solution.py:30
  488.8 9.4 %collective-permute-start.43 = (f32[4,4]{1,0:T(4,128)S(1)}, f32[4,4]{1,0:T(4,128)S(1)}, u32[]{:S(2)}, u32[]{:S(2)}) collective-permute-start(f32[4,4]{1,0:T(4,128)S(1)} %add.254), channel_id=1, source_target_pairs={{0,16},{1,17},{2,18},{3,19},{4,20},{5,21},{6,22},{7,23},{8,24},{9,... | collective-permute-start | bytes 200 | tf_op jit(solution)/shard_map/ppermute | solution.py:30
  498.2 14.4 %collective-permute-start.44 = (f32[4,4]{1,0:T(4,128)S(1)}, f32[4,4]{1,0:T(4,128)S(1)}, u32[]{:S(2)}, u32[]{:S(2)}) collective-permute-start(f32[4,4]{1,0:T(4,128)S(1)} %add.255), channel_id=1, source_target_pairs={{0,32},{1,33},{2,34},{3,35},{4,36},{5,37},{6,38},{7,39},{8,40},{9,... | collective-permute-start | bytes 200 | tf_op jit(solution)/shard_map/ppermute | solution.py:30
  (4 other events, 112.8 us)
Sparse Core Ops, SparseCore 0:
  10.0 53.0 all-gather.2
  404.7 42.9 reduce-scatter.1
where the time goes:
time: 522 us; the launch traced here: 520 us
  waiting for transfers between devices  257 us (49%)
  starting transfers between devices  207 us (40%)
  matrix products  22.8 us (4%)
  between operations  14.7 us (3%)
  local copies, waits for them, and re-layouts  14 us (3%)
    ppermute x39, starting transfers between devices, tree_sum(): value = value + lax.ppermute(value, axis, pairs)  194 us
    ppermute x39, waiting for transfers between devices, tree_sum(): value = value + lax.ppermute(value, axis, pairs)  94.4 us
    ppermute x3, waiting for transfers between devices, padded_2(): lax.ppermute(lax.slice_in_dim(block, 0, width, axis=dim), axis, backward)  62.7 us
    all_gather x1, waiting for transfers between devices, local(): psi_all = lax.all_gather(psi_flat, 'band', axis=0, tiled=True)  50.8 us
    reduce_scatter x1, waiting for transfers between devices, local(): lax.psum_scatter(partial_grid, 'band', scatter_dimension=2, tiled=True)  42.3 us
    dot_general x5, matrix products, project_slab(): jnp.dot(psi_all, vectors.T, precision=highest, preferred_element_type=jnp...  13.1 us
  transfers between devices with their start and end apart: 47, of which 46 were waited for; matrix products, arithmetic and copies ran while one was open for 2% of the time, Pallas kernels for 0%

commit v1 on v0

--- a/solution.py
+++ b/solution.py
@@ -66,7 +66,9 @@
     highest = lax.Precision.HIGHEST
     trial_slice = lax.dynamic_slice_in_dim(trials, band_index * y_share, y_share, 2)
     psi_flat = orbitals.reshape(nb_dev, cell_count)
-    psi_all = lax.all_gather(psi_flat, "band", axis=0, tiled=True)
+    psi_all = jnp.concatenate(
+        lax.all_to_all(jnp.stack([psi_flat] * lax.axis_size("band")), "band", 0, 0), axis=0
+    )
 
     def project_slab(vectors):
         intersection = jnp.dot(

time: 522 us -> 504 us (0.966)
  waiting for transfers between devices: 257 us -> 233 us
  starting transfers between devices: 207 us -> 214 us
    all_gather x1 -> x0, waiting for transfers between devices: 50.8 us -> none  [local(): psi_all = lax.all_gather(psi_flat, 'band', axis=0, tiled=True)]
    all_to_all x0 -> x1, waiting for transfers between devices: none -> 25.1 us  [local(): lax.all_to_all(jnp.stack([psi_flat] * lax.axis_size('band')), 'band', 0, 0)]
    unnamed x16, local copies, waits for them, and re-layouts: 8.04 us -> 2.49 us
    all_to_all x0 -> x1, starting transfers between devices: none -> 5.24 us  [local(): lax.all_to_all(jnp.stack([psi_flat] * lax.axis_size('band')), 'band', 0, 0)]
  transfers between devices with their start and end apart: 47 -> 47, of which waited for: 46 -> 46; matrix products, arithmetic and copies ran while one was open for 2% -> 1% of each run, Pallas kernels for 0% -> 0%
where the time goes in v1:
time: 504 us; the launch traced here: 502 us
  waiting for transfers between devices  233 us (46%)
  starting transfers between devices  214 us (42%)
  matrix products  22.8 us (5%)
  between operations  14.7 us (3%)
  local copies, waits for them, and re-layouts  13.1 us (3%)
    ppermute x39, starting transfers between devices, tree_sum(): value = value + lax.ppermute(value, axis, pairs)  196 us
    ppermute x39, waiting for transfers between devices, tree_sum(): value = value + lax.ppermute(value, axis, pairs)  95.6 us
    ppermute x3, waiting for transfers between devices, padded_2(): lax.ppermute(lax.slice_in_dim(block, 0, width, axis=dim), axis, backward)  62.7 us
    reduce_scatter x1, waiting for transfers between devices, local(): lax.psum_scatter(partial_grid, 'band', scatter_dimension=2, tiled=True)  43.3 us
    all_to_all x1, waiting for transfers between devices, local(): lax.all_to_all(jnp.stack([psi_flat] * lax.axis_size('band')), 'band', 0, 0)  25.1 us
    dot_general x5, matrix products, project_slab(): jnp.dot(psi_all, vectors.T, precision=highest, preferred_element_type=jnp...  13.1 us
  transfers between devices with their start and end apart: 47, of which 46 were waited for; matrix products, arithmetic and copies ran while one was open for 1% of the time, Pallas kernels for 0%

profile of v1, /device:TPU:4, one launch (start us, length us, event | category | flops | bytes accessed | tf_op | source)
XLA Modules:
  0.0 502.5 jit_solution(18177670900014711793)
XLA Ops:
  10.2 5.2 %all-to-all-start = ((f32[8,2,32768]{2,1,0:T(2,128)}), f32[8,2,32768]{2,1,0:T(2,128)}, u32[]{:S(2)}, u32[]{:S(2)}) async-start(f32[8,2,32768]{2,1,0:T(2,128)} %stack.3), calls=%async_computation | async-start | bytes 4194304 | tf_op jit(solution)/shard_map/all_to_all | solution.py:70
  16.5 25.1 %all-to-all-done = f32[8,2,32768]{2,1,0:T(2,128)} async-done(((f32[8,2,32768]{2,1,0:T(2,128)}), f32[8,2,32768]{2,1,0:T(2,128)}, u32[]{:S(2)}, u32[]{:S(2)}) %all-to-all-start) | async-done | bytes 2097184 | tf_op jit(solution)/shard_map/all_to_all | solution.py:70
  52.7 4.3 collective-permute-done.1
  57.0 3.8 collective-permute-start.2
  62.4 5.2 %collective-permute-start.3 = (f32[16,8]{0,1:T(8,128)S(1)}, f32[16,8]{0,1:T(8,128)S(1)}, u32[]{:S(2)}, u32[]{:S(2)}) collective-permute-start(f32[16,8]{0,1:T(8,128)S(1)} %add.198), channel_id=1, source_target_pairs={{0,8},{1,9},{2,10},{3,11},{4,12},{5,13},{6,14},{7,15},{8,0},{9,1},... | collective-permute-start | bytes 1544 | tf_op jit(solution)/shard_map/ppermute | solution.py:30
  69.2 9.1 %collective-permute-start.4 = (f32[16,8]{0,1:T(8,128)S(1)}, f32[16,8]{0,1:T(8,128)S(1)}, u32[]{:S(2)}, u32[]{:S(2)}) collective-permute-start(f32[16,8]{0,1:T(8,128)S(1)} %add.199), channel_id=1, source_target_pairs={{0,16},{1,17},{2,18},{3,19},{4,20},{5,21},{6,22},{7,23},{8,24},{9,... | collective-permute-start | bytes 1544 | tf_op jit(solution)/shard_map/ppermute | solution.py:30
  79.9 14.1 %collective-permute-start.5 = (f32[16,8]{0,1:T(8,128)S(1)}, f32[16,8]{0,1:T(8,128)S(1)}, u32[]{:S(2)}, u32[]{:S(2)}) collective-permute-start(f32[16,8]{0,1:T(8,128)S(1)} %add.200), channel_id=1, source_target_pairs={{0,32},{1,33},{2,34},{3,35},{4,36},{5,37},{6,38},{7,39},{8,40},{9,... | collective-permute-start | bytes 1544 | tf_op jit(solution)/shard_map/ppermute | solution.py:30
  107.7 4.3 collective-permute-done.7
  112.0 2.9 collective-permute-start.8
  117.5 3.4 collective-permute-start.9
  120.9 3.0 collective-permute-done.9
  123.9 5.0 collective-permute-start.10
  128.9 4.4 collective-permute-done.10
  133.3 11.2 %collective-permute-start.11 = (f32[16,8]{0,1:T(8,128)S(1)}, f32[16,8]{0,1:T(8,128)S(1)}, u32[]{:S(2)}, u32[]{:S(2)}) collective-permute-start(f32[16,8]{0,1:T(8,128)S(1)} %add.209), channel_id=1, source_target_pairs={{0,32},{1,33},{2,34},{3,35},{4,36},{5,37},{6,38},{7,39},{8,40},{9,... | collective-permute-start | bytes 1544 | tf_op jit(solution)/shard_map/ppermute | solution.py:30
  144.5 3.0 collective-permute-done.11
  153.3 20.8 %collective-permute-done.12 = f32[8,1,128,256]{3,0,2,1:T(8,128)S(1)} collective-permute-done((f32[8,1,128,256]{3,0,2,1:T(8,128)S(1)}, f32[8,1,128,256]{3,0,2,1:T(8,128)S(1)}, u32[]{:S(2)}, u32[]{:S(2)}) %collective-permute-start.12) | collective-permute-done | bytes 1048608 | tf_op jit(solution)/shard_map/ppermute | solution.py:19
  182.2 3.7 collective-permute-start.15
  185.9 3.3 collective-permute-done.15
  189.2 2.9 collective-permute-start.16
  194.7 3.4 collective-permute-start.17
  198.1 3.0 collective-permute-done.17
  201.1 7.0 %collective-permute-start.18 = (f32[16,8]{0,1:T(8,128)S(1)}, f32[16,8]{0,1:T(8,128)S(1)}, u32[]{:S(2)}, u32[]{:S(2)}) collective-permute-start(f32[16,8]{0,1:T(8,128)S(1)} %add.219), channel_id=1, source_target_pairs={{0,16},{1,17},{2,18},{3,19},{4,20},{5,21},{6,22},{7,23},{8,24},{9,... | collective-permute-start | bytes 1544 | tf_op jit(solution)/shard_map/ppermute | solution.py:30
  210.5 11.2 %collective-permute-start.19 = (f32[16,8]{0,1:T(8,128)S(1)}, f32[16,8]{0,1:T(8,128)S(1)}, u32[]{:S(2)}, u32[]{:S(2)}) collective-permute-start(f32[16,8]{0,1:T(8,128)S(1)} %add.220), channel_id=1, source_target_pairs={{0,32},{1,33},{2,34},{3,35},{4,36},{5,37},{6,38},{7,39},{8,40},{9,... | collective-permute-start | bytes 1544 | tf_op jit(solution)/shard_map/ppermute | solution.py:30
  221.7 3.0 collective-permute-done.19
  230.5 21.0 %collective-permute-done.20 = f32[8,1,128,256]{3,0,2,1:T(8,128)S(1)} collective-permute-done((f32[8,1,128,256]{3,0,2,1:T(8,128)S(1)}, f32[8,1,128,256]{3,0,2,1:T(8,128)S(1)}, u32[]{:S(2)}, u32[]{:S(2)}) %collective-permute-start.20) | collective-permute-done | bytes 1048608 | tf_op jit(solution)/shard_map/ppermute | solution.py:19
  263.2 4.3 collective-permute-done.23
  267.5 2.9 collective-permute-start.24
  273.0 3.4 collective-permute-start.25
  276.4 3.0 collective-permute-done.25
  279.4 7.0 %collective-permute-start.26 = (f32[16,8]{0,1:T(8,128)S(1)}, f32[16,8]{0,1:T(8,128)S(1)}, u32[]{:S(2)}, u32[]{:S(2)}) collective-permute-start(f32[16,8]{0,1:T(8,128)S(1)} %add.231), channel_id=1, source_target_pairs={{0,16},{1,17},{2,18},{3,19},{4,20},{5,21},{6,22},{7,23},{8,24},{9,... | collective-permute-start | bytes 1544 | tf_op jit(solution)/shard_map/ppermute | solution.py:30
  288.8 11.2 %collective-permute-start.27 = (f32[16,8]{0,1:T(8,128)S(1)}, f32[16,8]{0,1:T(8,128)S(1)}, u32[]{:S(2)}, u32[]{:S(2)}) collective-permute-start(f32[16,8]{0,1:T(8,128)S(1)} %add.232), channel_id=1, source_target_pairs={{0,32},{1,33},{2,34},{3,35},{4,36},{5,37},{6,38},{7,39},{8,40},{9,... | collective-permute-start | bytes 1544 | tf_op jit(solution)/shard_map/ppermute | solution.py:30
  300.0 3.0 collective-permute-done.27
  308.8 21.0 %collective-permute-done.28 = f32[8,1,128,256]{3,0,2,1:T(8,128)S(1)} collective-permute-done((f32[8,1,128,256]{3,0,2,1:T(8,128)S(1)}, f32[8,1,128,256]{3,0,2,1:T(8,128)S(1)}, u32[]{:S(2)}, u32[]{:S(2)}) %collective-permute-start.28) | collective-permute-done | bytes 1048608 | tf_op jit(solution)/shard_map/ppermute | solution.py:19
  338.0 3.5 collective-permute-start.31
  341.5 3.5 collective-permute-done.31
  345.0 3.4 collective-permute-start.32
  350.5 5.0 collective-permute-start.33
  357.1 7.6 %collective-permute-start.34 = (f32[16,8]{0,1:T(8,128)S(1)}, f32[16,8]{0,1:T(8,128)S(1)}, u32[]{:S(2)}, u32[]{:S(2)}) collective-permute-start(f32[16,8]{0,1:T(8,128)S(1)} %add.243), channel_id=1, source_target_pairs={{0,16},{1,17},{2,18},{3,19},{4,20},{5,21},{6,22},{7,23},{8,24},{9,... | collective-permute-start | bytes 1544 | tf_op jit(solution)/shard_map/ppermute | solution.py:30
  366.5 10.9 %collective-permute-start.35 = (f32[16,8]{0,1:T(8,128)S(1)}, f32[16,8]{0,1:T(8,128)S(1)}, u32[]{:S(2)}, u32[]{:S(2)}) collective-permute-start(f32[16,8]{0,1:T(8,128)S(1)} %add.244), channel_id=1, source_target_pairs={{0,32},{1,33},{2,34},{3,35},{4,36},{5,37},{6,38},{7,39},{8,40},{9,... | collective-permute-start | bytes 1544 | tf_op jit(solution)/shard_map/ppermute | solution.py:30
  386.9 43.3 %reduce-scatter.2.cloned.1.call-done = f32[4,1,16,256]{3,2,1,0:T(8,128)} async-done(((f32[4,1,128,256]{3,2,1,0:T(8,128)}), f32[4,1,16,256]{3,2,1,0:T(8,128)}) %reduce-scatter.2.cloned.1.call-update) | async-done | bytes 65552 | tf_op jit(solution)/shard_map/reduce_scatter | solution.py:102
  433.4 3.6 collective-permute-done.36
  437.0 2.8 collective-permute-start.37
  439.7 4.2 collective-permute-done.37
  455.2 4.3 collective-permute-done.40
  459.4 3.5 collective-permute-start.41
  464.9 4.4 collective-permute-start.42
  471.3 7.6 %collective-permute-start.43 = (f32[4,4]{1,0:T(4,128)S(1)}, f32[4,4]{1,0:T(4,128)S(1)}, u32[]{:S(2)}, u32[]{:S(2)}) collective-permute-start(f32[4,4]{1,0:T(4,128)S(1)} %add.254), channel_id=1, source_target_pairs={{0,16},{1,17},{2,18},{3,19},{4,20},{5,21},{6,22},{7,23},{8,24},{9,... | collective-permute-start | bytes 200 | tf_op jit(solution)/shard_map/ppermute | solution.py:30
  480.7 12.8 %collective-permute-start.44 = (f32[4,4]{1,0:T(4,128)S(1)}, f32[4,4]{1,0:T(4,128)S(1)}, u32[]{:S(2)}, u32[]{:S(2)}) collective-permute-start(f32[4,4]{1,0:T(4,128)S(1)} %add.255), channel_id=1, source_target_pairs={{0,32},{1,33},{2,34},{3,35},{4,36},{5,37},{6,38},{7,39},{8,40},{9,... | collective-permute-start | bytes 200 | tf_op jit(solution)/shard_map/ppermute | solution.py:30
  (131 shorter events, 128.5 us)
Async XLA Ops:
  10.2 31.4 %all-to-all-start = ((f32[8,2,32768]{2,1,0:T(2,128)}), f32[8,2,32768]{2,1,0:T(2,128)}, u32[]{:S(2)}, u32[]{:S(2)}) async-start(f32[8,2,32768]{2,1,0:T(2,128)} %stack.3), calls=%async_computation | async-start | bytes 4194304 | tf_op jit(solution)/shard_map/all_to_all | solution.py:70
  15.5 414.7 %reduce-scatter.2.cloned.1.call-start = ((), (), s32[]{:S(2)}) async-start(), calls=%async_computation.2 | async-start | bytes 589824 | tf_op jit(solution)/shard_map/reduce_scatter | solution.py:102
  44.3 49.6 %copy-start.4 = (f32[2]{0:T(128)S(1)}, f32[2]{0:T(128)}, u32[]{:S(2)}) copy-start(f32[2]{0:T(128)} %param.6) | copy-start | bytes 28
  46.9 3.1 collective-permute-start
  50.0 7.0 %collective-permute-start.1 = (f32[16,8]{0,1:T(8,128)S(1)}, f32[16,8]{0,1:T(8,128)S(1)}, u32[]{:S(2)}, u32[]{:S(2)}) collective-permute-start(f32[16,8]{0,1:T(8,128)S(1)} %add.196), channel_id=1, source_target_pairs={{0,2},{1,3},{2,0},{3,1},{4,6},{5,7},{6,4},{7,5},{8,10},{9,11},{10,... | collective-permute-start | bytes 1544 | tf_op jit(solution)/shard_map/ppermute | solution.py:30
  57.0 5.5 %collective-permute-start.2 = (f32[16,8]{0,1:T(8,128)S(1)}, f32[16,8]{0,1:T(8,128)S(1)}, u32[]{:S(2)}, u32[]{:S(2)}) collective-permute-start(f32[16,8]{0,1:T(8,128)S(1)} %add.197), channel_id=1, source_target_pairs={{0,4},{1,5},{2,6},{3,7},{4,0},{5,1},{6,2},{7,3},{8,12},{9,13},{10,... | collective-permute-start | bytes 1544 | tf_op jit(solution)/shard_map/ppermute | solution.py:30
  62.4 6.7 %collective-permute-start.3 = (f32[16,8]{0,1:T(8,128)S(1)}, f32[16,8]{0,1:T(8,128)S(1)}, u32[]{:S(2)}, u32[]{:S(2)}) collective-permute-start(f32[16,8]{0,1:T(8,128)S(1)} %add.198), channel_id=1, source_target_pairs={{0,8},{1,9},{2,10},{3,11},{4,12},{5,13},{6,14},{7,15},{8,0},{9,1},... | collective-permute-start | bytes 1544 | tf_op jit(solution)/shard_map/ppermute | solution.py:30
  69.2 10.7 %collective-permute-start.4 = (f32[16,8]{0,1:T(8,128)S(1)}, f32[16,8]{0,1:T(8,128)S(1)}, u32[]{:S(2)}, u32[]{:S(2)}) collective-permute-start(f32[16,8]{0,1:T(8,128)S(1)} %add.199), channel_id=1, source_target_pairs={{0,16},{1,17},{2,18},{3,19},{4,20},{5,21},{6,22},{7,23},{8,24},{9,... | collective-permute-start | bytes 1544 | tf_op jit(solution)/shard_map/ppermute | solution.py:30
  79.9 17.0 %collective-permute-start.5 = (f32[16,8]{0,1:T(8,128)S(1)}, f32[16,8]{0,1:T(8,128)S(1)}, u32[]{:S(2)}, u32[]{:S(2)}) collective-permute-start(f32[16,8]{0,1:T(8,128)S(1)} %add.200), channel_id=1, source_target_pairs={{0,32},{1,33},{2,34},{3,35},{4,36},{5,37},{6,38},{7,39},{8,40},{9,... | collective-permute-start | bytes 1544 | tf_op jit(solution)/shard_map/ppermute | solution.py:30
  101.9 3.1 collective-permute-start.6
  105.0 7.0 %collective-permute-start.7 = (f32[16,8]{0,1:T(8,128)S(1)}, f32[16,8]{0,1:T(8,128)S(1)}, u32[]{:S(2)}, u32[]{:S(2)}) collective-permute-start(f32[16,8]{0,1:T(8,128)S(1)} %add.205), channel_id=1, source_target_pairs={{0,2},{1,3},{2,0},{3,1},{4,6},{5,7},{6,4},{7,5},{8,10},{9,11},{10,... | collective-permute-start | bytes 1544 | tf_op jit(solution)/shard_map/ppermute | solution.py:30
  112.0 5.5 %collective-permute-start.8 = (f32[16,8]{0,1:T(8,128)S(1)}, f32[16,8]{0,1:T(8,128)S(1)}, u32[]{:S(2)}, u32[]{:S(2)}) collective-permute-start(f32[16,8]{0,1:T(8,128)S(1)} %add.206), channel_id=1, source_target_pairs={{0,4},{1,5},{2,6},{3,7},{4,0},{5,1},{6,2},{7,3},{8,12},{9,13},{10,... | collective-permute-start | bytes 1544 | tf_op jit(solution)/shard_map/ppermute | solution.py:30
  117.5 6.4 %collective-permute-start.9 = (f32[16,8]{0,1:T(8,128)S(1)}, f32[16,8]{0,1:T(8,128)S(1)}, u32[]{:S(2)}, u32[]{:S(2)}) collective-permute-start(f32[16,8]{0,1:T(8,128)S(1)} %add.207), channel_id=1, source_target_pairs={{0,8},{1,9},{2,10},{3,11},{4,12},{5,13},{6,14},{7,15},{8,0},{9,1},... | collective-permute-start | bytes 1544 | tf_op jit(solution)/shard_map/ppermute | solution.py:30
  123.9 9.4 %collective-permute-start.10 = (f32[16,8]{0,1:T(8,128)S(1)}, f32[16,8]{0,1:T(8,128)S(1)}, u32[]{:S(2)}, u32[]{:S(2)}) collective-permute-start(f32[16,8]{0,1:T(8,128)S(1)} %add.208), channel_id=1, source_target_pairs={{0,16},{1,17},{2,18},{3,19},{4,20},{5,21},{6,22},{7,23},{8,24},{9,... | collective-permute-start | bytes 1544 | tf_op jit(solution)/shard_map/ppermute | solution.py:30
  133.3 14.2 %collective-permute-start.11 = (f32[16,8]{0,1:T(8,128)S(1)}, f32[16,8]{0,1:T(8,128)S(1)}, u32[]{:S(2)}, u32[]{:S(2)}) collective-permute-start(f32[16,8]{0,1:T(8,128)S(1)} %add.209), channel_id=1, source_target_pairs={{0,32},{1,33},{2,34},{3,35},{4,36},{5,37},{6,38},{7,39},{8,40},{9,... | collective-permute-start | bytes 1544 | tf_op jit(solution)/shard_map/ppermute | solution.py:30
  148.6 25.5 %collective-permute-start.12 = (f32[8,1,128,256]{3,0,2,1:T(8,128)S(1)}, f32[8,1,128,256]{3,0,2,1:T(8,128)S(1)}, u32[]{:S(2)}, u32[]{:S(2)}) collective-permute-start(f32[8,1,128,256]{3,0,2,1:T(8,128)S(1)} %bitcast.53), channel_id=1, source_target_pairs={{1,0},{2,1},{3,2},{4,3},{5,4},{6,5},{7,6},{8,7},{9,8},{10,9},{11,1... | collective-permute-start | bytes 3145736 | tf_op jit(solution)/shard_map/ppermute | solution.py:19
  150.6 25.2 %collective-permute-start.13 = (f32[8,1,128,256]{3,0,2,1:T(8,128)S(1)}, f32[8,1,128,256]{3,0,2,1:T(8,128)S(1)}, u32[]{:S(2)}, u32[]{:S(2)}) collective-permute-start(f32[8,1,128,256]{3,0,2,1:T(8,128)S(1)} %bitcast.54), channel_id=1, source_target_pairs={{0,1},{1,2},{2,3},{3,4},{4,5},{5,6},{6,7},{7,8},{8,9},{9,10},{10,1... | collective-permute-start | bytes 3145736 | tf_op jit(solution)/shard_map/ppermute | solution.py:16
  179.1 3.1 collective-permute-start.14
  182.2 7.0 %collective-permute-start.15 = (f32[16,8]{0,1:T(8,128)S(1)}, f32[16,8]{0,1:T(8,128)S(1)}, u32[]{:S(2)}, u32[]{:S(2)}) collective-permute-start(f32[16,8]{0,1:T(8,128)S(1)} %add.216), channel_id=1, source_target_pairs={{0,2},{1,3},{2,0},{3,1},{4,6},{5,7},{6,4},{7,5},{8,10},{9,11},{10,... | collective-permute-start | bytes 1544 | tf_op jit(solution)/shard_map/ppermute | solution.py:30
  189.2 5.5 %collective-permute-start.16 = (f32[16,8]{0,1:T(8,128)S(1)}, f32[16,8]{0,1:T(8,128)S(1)}, u32[]{:S(2)}, u32[]{:S(2)}) collective-permute-start(f32[16,8]{0,1:T(8,128)S(1)} %add.217), channel_id=1, source_target_pairs={{0,4},{1,5},{2,6},{3,7},{4,0},{5,1},{6,2},{7,3},{8,12},{9,13},{10,... | collective-permute-start | bytes 1544 | tf_op jit(solution)/shard_map/ppermute | solution.py:30
  194.7 6.4 %collective-permute-start.17 = (f32[16,8]{0,1:T(8,128)S(1)}, f32[16,8]{0,1:T(8,128)S(1)}, u32[]{:S(2)}, u32[]{:S(2)}) collective-permute-start(f32[16,8]{0,1:T(8,128)S(1)} %add.218), channel_id=1, source_target_pairs={{0,8},{1,9},{2,10},{3,11},{4,12},{5,13},{6,14},{7,15},{8,0},{9,1},... | collective-permute-start | bytes 1544 | tf_op jit(solution)/shard_map/ppermute | solution.py:30
  201.1 9.4 %collective-permute-start.18 = (f32[16,8]{0,1:T(8,128)S(1)}, f32[16,8]{0,1:T(8,128)S(1)}, u32[]{:S(2)}, u32[]{:S(2)}) collective-permute-start(f32[16,8]{0,1:T(8,128)S(1)} %add.219), channel_id=1, source_target_pairs={{0,16},{1,17},{2,18},{3,19},{4,20},{5,21},{6,22},{7,23},{8,24},{9,... | collective-permute-start | bytes 1544 | tf_op jit(solution)/shard_map/ppermute | solution.py:30
  210.5 14.2 %collective-permute-start.19 = (f32[16,8]{0,1:T(8,128)S(1)}, f32[16,8]{0,1:T(8,128)S(1)}, u32[]{:S(2)}, u32[]{:S(2)}) collective-permute-start(f32[16,8]{0,1:T(8,128)S(1)} %add.220), channel_id=1, source_target_pairs={{0,32},{1,33},{2,34},{3,35},{4,36},{5,37},{6,38},{7,39},{8,40},{9,... | collective-permute-start | bytes 1544 | tf_op jit(solution)/shard_map/ppermute | solution.py:30
  226.0 25.5 %collective-permute-start.20 = (f32[8,1,128,256]{3,0,2,1:T(8,128)S(1)}, f32[8,1,128,256]{3,0,2,1:T(8,128)S(1)}, u32[]{:S(2)}, u32[]{:S(2)}) collective-permute-start(f32[8,1,128,256]{3,0,2,1:T(8,128)S(1)} %bitcast.58), channel_id=1, source_target_pairs={{1,0},{2,1},{3,2},{4,3},{5,4},{6,5},{7,6},{8,7},{9,8},{10,9},{11,1... | collective-permute-start | bytes 3145736 | tf_op jit(solution)/shard_map/ppermute | solution.py:19
  227.9 26.2 %collective-permute-start.21 = (f32[8,1,128,256]{3,0,2,1:T(8,128)S(1)}, f32[8,1,128,256]{3,0,2,1:T(8,128)S(1)}, u32[]{:S(2)}, u32[]{:S(2)}) collective-permute-start(f32[8,1,128,256]{3,0,2,1:T(8,128)S(1)} %bitcast.59), channel_id=1, source_target_pairs={{0,1},{1,2},{2,3},{3,4},{4,5},{5,6},{6,7},{7,8},{8,9},{9,10},{10,1... | collective-permute-start | bytes 3145736 | tf_op jit(solution)/shard_map/ppermute | solution.py:16
  257.4 3.1 collective-permute-start.22
  260.5 7.0 %collective-permute-start.23 = (f32[16,8]{0,1:T(8,128)S(1)}, f32[16,8]{0,1:T(8,128)S(1)}, u32[]{:S(2)}, u32[]{:S(2)}) collective-permute-start(f32[16,8]{0,1:T(8,128)S(1)} %add.228), channel_id=1, source_target_pairs={{0,2},{1,3},{2,0},{3,1},{4,6},{5,7},{6,4},{7,5},{8,10},{9,11},{10,... | collective-permute-start | bytes 1544 | tf_op jit(solution)/shard_map/ppermute | solution.py:30
  267.5 5.5 %collective-permute-start.24 = (f32[16,8]{0,1:T(8,128)S(1)}, f32[16,8]{0,1:T(8,128)S(1)}, u32[]{:S(2)}, u32[]{:S(2)}) collective-permute-start(f32[16,8]{0,1:T(8,128)S(1)} %add.229), channel_id=1, source_target_pairs={{0,4},{1,5},{2,6},{3,7},{4,0},{5,1},{6,2},{7,3},{8,12},{9,13},{10,... | collective-permute-start | bytes 1544 | tf_op jit(solution)/shard_map/ppermute | solution.py:30
  273.0 6.4 %collective-permute-start.25 = (f32[16,8]{0,1:T(8,128)S(1)}, f32[16,8]{0,1:T(8,128)S(1)}, u32[]{:S(2)}, u32[]{:S(2)}) collective-permute-start(f32[16,8]{0,1:T(8,128)S(1)} %add.230), channel_id=1, source_target_pairs={{0,8},{1,9},{2,10},{3,11},{4,12},{5,13},{6,14},{7,15},{8,0},{9,1},... | collective-permute-start | bytes 1544 | tf_op jit(solution)/shard_map/ppermute | solution.py:30
  279.4 9.4 %collective-permute-start.26 = (f32[16,8]{0,1:T(8,128)S(1)}, f32[16,8]{0,1:T(8,128)S(1)}, u32[]{:S(2)}, u32[]{:S(2)}) collective-permute-start(f32[16,8]{0,1:T(8,128)S(1)} %add.231), channel_id=1, source_target_pairs={{0,16},{1,17},{2,18},{3,19},{4,20},{5,21},{6,22},{7,23},{8,24},{9,... | collective-permute-start | bytes 1544 | tf_op jit(solution)/shard_map/ppermute | solution.py:30
  288.8 14.2 %collective-permute-start.27 = (f32[16,8]{0,1:T(8,128)S(1)}, f32[16,8]{0,1:T(8,128)S(1)}, u32[]{:S(2)}, u32[]{:S(2)}) collective-permute-start(f32[16,8]{0,1:T(8,128)S(1)} %add.232), channel_id=1, source_target_pairs={{0,32},{1,33},{2,34},{3,35},{4,36},{5,37},{6,38},{7,39},{8,40},{9,... | collective-permute-start | bytes 1544 | tf_op jit(solution)/shard_map/ppermute | solution.py:30
  304.3 25.5 %collective-permute-start.28 = (f32[8,1,128,256]{3,0,2,1:T(8,128)S(1)}, f32[8,1,128,256]{3,0,2,1:T(8,128)S(1)}, u32[]{:S(2)}, u32[]{:S(2)}) collective-permute-start(f32[8,1,128,256]{3,0,2,1:T(8,128)S(1)} %bitcast.48), channel_id=1, source_target_pairs={{1,0},{2,1},{3,2},{4,3},{5,4},{6,5},{7,6},{8,7},{9,8},{10,9},{11,1... | collective-permute-start | bytes 3145736 | tf_op jit(solution)/shard_map/ppermute | solution.py:19
  306.2 25.4 %collective-permute-start.29 = (f32[8,1,128,256]{3,0,2,1:T(8,128)S(1)}, f32[8,1,128,256]{3,0,2,1:T(8,128)S(1)}, u32[]{:S(2)}, u32[]{:S(2)}) collective-permute-start(f32[8,1,128,256]{3,0,2,1:T(8,128)S(1)} %bitcast.49), channel_id=1, source_target_pairs={{0,1},{1,2},{2,3},{3,4},{4,5},{5,6},{6,7},{7,8},{8,9},{9,10},{10,1... | collective-permute-start | bytes 3145736 | tf_op jit(solution)/shard_map/ppermute | solution.py:16
  334.9 3.1 collective-permute-start.30
  338.0 7.0 %collective-permute-start.31 = (f32[16,8]{0,1:T(8,128)S(1)}, f32[16,8]{0,1:T(8,128)S(1)}, u32[]{:S(2)}, u32[]{:S(2)}) collective-permute-start(f32[16,8]{0,1:T(8,128)S(1)} %add.240), channel_id=1, source_target_pairs={{0,2},{1,3},{2,0},{3,1},{4,6},{5,7},{6,4},{7,5},{8,10},{9,11},{10,... | collective-permute-start | bytes 1544 | tf_op jit(solution)/shard_map/ppermute | solution.py:30
  345.0 5.5 %collective-permute-start.32 = (f32[16,8]{0,1:T(8,128)S(1)}, f32[16,8]{0,1:T(8,128)S(1)}, u32[]{:S(2)}, u32[]{:S(2)}) collective-permute-start(f32[16,8]{0,1:T(8,128)S(1)} %add.241), channel_id=1, source_target_pairs={{0,4},{1,5},{2,6},{3,7},{4,0},{5,1},{6,2},{7,3},{8,12},{9,13},{10,... | collective-permute-start | bytes 1544 | tf_op jit(solution)/shard_map/ppermute | solution.py:30
  350.5 6.6 %collective-permute-start.33 = (f32[16,8]{0,1:T(8,128)S(1)}, f32[16,8]{0,1:T(8,128)S(1)}, u32[]{:S(2)}, u32[]{:S(2)}) collective-permute-start(f32[16,8]{0,1:T(8,128)S(1)} %add.242), channel_id=1, source_target_pairs={{0,8},{1,9},{2,10},{3,11},{4,12},{5,13},{6,14},{7,15},{8,0},{9,1},... | collective-permute-start | bytes 1544 | tf_op jit(solution)/shard_map/ppermute | solution.py:30
  357.1 9.4 %collective-permute-start.34 = (f32[16,8]{0,1:T(8,128)S(1)}, f32[16,8]{0,1:T(8,128)S(1)}, u32[]{:S(2)}, u32[]{:S(2)}) collective-permute-start(f32[16,8]{0,1:T(8,128)S(1)} %add.243), channel_id=1, source_target_pairs={{0,16},{1,17},{2,18},{3,19},{4,20},{5,21},{6,22},{7,23},{8,24},{9,... | collective-permute-start | bytes 1544 | tf_op jit(solution)/shard_map/ppermute | solution.py:30
  366.5 14.2 %collective-permute-start.35 = (f32[16,8]{0,1:T(8,128)S(1)}, f32[16,8]{0,1:T(8,128)S(1)}, u32[]{:S(2)}, u32[]{:S(2)}) collective-permute-start(f32[16,8]{0,1:T(8,128)S(1)} %add.244), channel_id=1, source_target_pairs={{0,32},{1,33},{2,34},{3,35},{4,36},{5,37},{6,38},{7,39},{8,40},{9,... | collective-permute-start | bytes 1544 | tf_op jit(solution)/shard_map/ppermute | solution.py:30
  431.4 5.5 %collective-permute-start.36 = (f32[4,4]{1,0:T(4,128)S(1)}, f32[4,4]{1,0:T(4,128)S(1)}, u32[]{:S(2)}, u32[]{:S(2)}) collective-permute-start(f32[4,4]{1,0:T(4,128)S(1)} %convolution_bitcast_fusion.5), channel_id=1, source_target_pairs={{0,64},{64,0},{128,192},{192,128},{256,320},{320,256},{384,448},{4... | collective-permute-start | bytes 200 | tf_op jit(solution)/shard_map/ppermute | solution.py:30
  437.0 7.0 %collective-permute-start.37 = (f32[4,4]{1,0:T(4,128)S(1)}, f32[4,4]{1,0:T(4,128)S(1)}, u32[]{:S(2)}, u32[]{:S(2)}) collective-permute-start(f32[4,4]{1,0:T(4,128)S(1)} %add.248), channel_id=1, source_target_pairs={{0,128},{64,192},{128,0},{192,64},{256,384},{320,448},{384,256},{4... | collective-permute-start | bytes 200 | tf_op jit(solution)/shard_map/ppermute | solution.py:30
  443.9 5.5 %collective-permute-start.38 = (f32[4,4]{1,0:T(4,128)S(1)}, f32[4,4]{1,0:T(4,128)S(1)}, u32[]{:S(2)}, u32[]{:S(2)}) collective-permute-start(f32[4,4]{1,0:T(4,128)S(1)} %add.249), channel_id=1, source_target_pairs={{0,256},{64,320},{128,384},{192,448},{256,0},{320,64},{384,128},{4... | collective-permute-start | bytes 200 | tf_op jit(solution)/shard_map/ppermute | solution.py:30
  449.4 3.0 collective-permute-start.39
  452.5 7.0 %collective-permute-start.40 = (f32[4,4]{1,0:T(4,128)S(1)}, f32[4,4]{1,0:T(4,128)S(1)}, u32[]{:S(2)}, u32[]{:S(2)}) collective-permute-start(f32[4,4]{1,0:T(4,128)S(1)} %add.251), channel_id=1, source_target_pairs={{0,2},{1,3},{2,0},{3,1},{4,6},{5,7},{6,4},{7,5},{8,10},{9,11},{10,... | collective-permute-start | bytes 200 | tf_op jit(solution)/shard_map/ppermute | solution.py:30
  459.4 5.5 %collective-permute-start.41 = (f32[4,4]{1,0:T(4,128)S(1)}, f32[4,4]{1,0:T(4,128)S(1)}, u32[]{:S(2)}, u32[]{:S(2)}) collective-permute-start(f32[4,4]{1,0:T(4,128)S(1)} %add.252), channel_id=1, source_target_pairs={{0,4},{1,5},{2,6},{3,7},{4,0},{5,1},{6,2},{7,3},{8,12},{9,13},{10,... | collective-permute-start | bytes 200 | tf_op jit(solution)/shard_map/ppermute | solution.py:30
  464.9 6.4 %collective-permute-start.42 = (f32[4,4]{1,0:T(4,128)S(1)}, f32[4,4]{1,0:T(4,128)S(1)}, u32[]{:S(2)}, u32[]{:S(2)}) collective-permute-start(f32[4,4]{1,0:T(4,128)S(1)} %add.253), channel_id=1, source_target_pairs={{0,8},{1,9},{2,10},{3,11},{4,12},{5,13},{6,14},{7,15},{8,0},{9,1},... | collective-permute-start | bytes 200 | tf_op jit(solution)/shard_map/ppermute | solution.py:30
  471.3 9.4 %collective-permute-start.43 = (f32[4,4]{1,0:T(4,128)S(1)}, f32[4,4]{1,0:T(4,128)S(1)}, u32[]{:S(2)}, u32[]{:S(2)}) collective-permute-start(f32[4,4]{1,0:T(4,128)S(1)} %add.254), channel_id=1, source_target_pairs={{0,16},{1,17},{2,18},{3,19},{4,20},{5,21},{6,22},{7,23},{8,24},{9,... | collective-permute-start | bytes 200 | tf_op jit(solution)/shard_map/ppermute | solution.py:30
  480.7 14.4 %collective-permute-start.44 = (f32[4,4]{1,0:T(4,128)S(1)}, f32[4,4]{1,0:T(4,128)S(1)}, u32[]{:S(2)}, u32[]{:S(2)}) collective-permute-start(f32[4,4]{1,0:T(4,128)S(1)} %add.255), channel_id=1, source_target_pairs={{0,32},{1,33},{2,34},{3,35},{4,36},{5,37},{6,38},{7,39},{8,40},{9,... | collective-permute-start | bytes 200 | tf_op jit(solution)/shard_map/ppermute | solution.py:30
  (5 other events, 101.1 us)
Sparse Core Ops, SparseCore 0:
  386.1 44.0 reduce-scatter.1
